TPU v7x, 32 devices: a whole 2x2x4 slice. The times are simulated.
32 devices in a mesh: parts: 2 (over x), wide: 16 (over z, y, core).
Axes of the slice: x: 2, y: 2, z: 4, core: 2. Of those that a mesh axis runs over, the one named last changes fastest.
Arguments:
- frames: float32 [65536, 80], P(('parts', 'wide')), parts along dimension 0, may hold values from -6 to 6
- seg_start: int32 [2048], P(('parts', 'wide')), parts along dimension 0, may hold values from 1 to 1983
- seg_dest: int32 [2048], P(('parts', 'wide')), parts along dimension 0, may hold values from -1 to 15, as said below
- rec_id: int32 [2048], P(('parts', 'wide')), parts along dimension 0, may hold values from 0 to 63
- conv_weight: float32 [240, 1024], replicated, may hold values from -0.375 to 0.375
- conv_bias: float32 [1024], replicated, may hold values from -0.5 to 0.5
- proj_weight: float32 [2048, 192], replicated, may hold values from -0.125 to 0.125
- smooth_kernel: float32 [3, 3], replicated, may hold values from 0.2 to 1
Outputs:
- smoothed: float32 [1024, 512], P(('parts', 'wide')), parts along dimension 0
There are 2 independent parts, one for each index of `parts`. A program takes and returns all parts, laid end to end along the dimension named above; an argument that names none is the same for every part. Nothing has to cross between parts.
Inputs may be any that keep to these rules, and one draw needn't show every extreme that they name: `seg_dest`: -1 marks an unused slot; on each device the used slots come first; at most 4 segments of one device go to one device, and some device reaches this; every device is assigned exactly 32 segments.
All inputs are finite; a program needn't handle non-finite values.
Results may differ from a plain program's by a relative error of at most 0.001.
Values may be sent and summed in bfloat16 or wider, within the bound.
No kernel may reach another device: no remote copies, remote signals or barrier semaphores. Data moves between devices by JAX's collectives and lax.ppermute only.
A program may use at most 64 MiB of HBM per device.

v0:
```python
import math
import jax
import jax.numpy as jnp
from jax import lax
from jax.sharding import PartitionSpec as P

FEAT = 80
CH = 1024
EMB = 192
SEGLEN = 64
SEG_DEV = 32
PRECISE = lax.Precision.HIGHEST
AFF_SCALE = 8.0


def pool_segments(windows, conv_weight, conv_bias, proj_weight):
    seg_total = windows.shape[0]
    block_size = math.gcd(seg_total, 16)
    grouped = windows.reshape(seg_total // block_size, block_size, SEGLEN + 2, FEAT)

    def one_block(win_block):
        stacked = jnp.concatenate(
            [win_block[:, 0:SEGLEN], win_block[:, 1 : SEGLEN + 1], win_block[:, 2 : SEGLEN + 2]],
            axis=2,
        )
        preact = jnp.dot(
            stacked.reshape(block_size * SEGLEN, 3 * FEAT),
            conv_weight,
            precision=PRECISE,
            preferred_element_type=jnp.float32,
        )
        activated = jax.nn.relu(preact + conv_bias).reshape(block_size, SEGLEN, CH)
        frame_mean = jnp.mean(activated, axis=1)
        deviation = activated - frame_mean[:, None, :]
        frame_std = jnp.sqrt(jnp.mean(deviation * deviation, axis=1) + 1e-05)
        return jnp.concatenate([frame_mean, frame_std], axis=1)

    pooled = lax.map(one_block, grouped).reshape(seg_total, 2 * CH)
    return jnp.dot(pooled, proj_weight, precision=PRECISE, preferred_element_type=jnp.float32)


def smooth_rows(padded_rows, smooth_kernel):
    padded = jnp.pad(padded_rows, ((0, 0), (1, 1)))
    height = padded.shape[0] - 2
    col_count = padded.shape[1] - 2
    result = jnp.zeros((height, col_count), padded.dtype)
    for row_off in range(3):
        for col_off in range(3):
            result = (
                result
                + smooth_kernel[row_off, col_off]
                * padded[row_off : row_off + height, col_off : col_off + col_count]
            )
    return result


def compact(arrived_rec):
    present = arrived_rec >= 0
    position = jnp.cumsum(present.astype(jnp.int32)) - 1
    selected = present[None, :] & (
        position[None, :] == jnp.arange(SEG_DEV, dtype=jnp.int32)[:, None]
    )
    seg_rec = jnp.sum(jnp.where(selected, arrived_rec[None, :], 0), axis=1).astype(jnp.int32)
    return (selected.astype(jnp.float32), seg_rec)


def score_panel(unit, seg_rec, panel_unit, panel_rec):
    scores = AFF_SCALE * jnp.dot(unit, panel_unit.T, preferred_element_type=jnp.float32)
    return jnp.where(seg_rec[:, None] == panel_rec[None, :], 0.0, scores)


def per_device(
    frames, seg_start, seg_dest, rec_id, conv_weight, conv_bias, proj_weight, smooth_kernel
):
    group_size = lax.axis_size("wide")
    slot_count = seg_dest.shape[0]
    pair_cap = -(-slot_count // group_size)
    matches = (seg_dest[None, :] == jnp.arange(group_size, dtype=jnp.int32)[:, None]).astype(
        jnp.int32
    )
    order_pos = jnp.sum(jnp.cumsum(matches, axis=1) * matches, axis=0) - 1
    target = jnp.where(seg_dest >= 0, seg_dest * pair_cap + order_pos, -1)
    table = target[None, :] == jnp.arange(group_size * pair_cap, dtype=jnp.int32)[:, None]
    router = table.astype(jnp.float32)
    send_rec = (jnp.sum(jnp.where(table, rec_id[None, :] + 1, 0), axis=1) - 1).reshape(
        group_size, pair_cap
    )

    def cut_one(offset):
        return lax.dynamic_slice_in_dim(frames, offset - 1, SEGLEN + 2, 0)

    windows = jax.vmap(cut_one)(seg_start)
    embedded = pool_segments(windows, conv_weight, conv_bias, proj_weight)
    outgoing = jnp.dot(router, embedded, precision=PRECISE).reshape(group_size, pair_cap, EMB)
    arrived, arrived_rec = (
        lax.all_to_all(outgoing, "wide", split_axis=0, concat_axis=0, tiled=True),
        lax.all_to_all(send_rec, "wide", split_axis=0, concat_axis=0, tiled=True),
    )
    selector, seg_rec = compact(arrived_rec.reshape(group_size * pair_cap))
    seg_rows = jnp.dot(selector, arrived.reshape(group_size * pair_cap, EMB), precision=PRECISE)
    mean_sum = lax.psum(jnp.sum(seg_rows, axis=0), "wide")
    centred = seg_rows - mean_sum / (SEG_DEV * group_size)
    unit = (centred / jnp.sqrt(jnp.sum(centred * centred, axis=1, keepdims=True) + 1e-06)).astype(
        jnp.bfloat16
    )
    total_rows = SEG_DEV * group_size
    all_rec = jnp.zeros((total_rows,), jnp.int32)
    kept_rec = all_rec
    panel_unit = lax.all_gather(unit, "wide", axis=0, tiled=True)
    panel_rec = lax.all_gather(seg_rec, "wide", axis=0, tiled=True)
    scores = score_panel(unit, seg_rec, panel_unit, panel_rec)
    affinity = scores
    kept_rec = lax.dynamic_update_slice_in_dim(kept_rec, panel_rec, jnp.int32(0), 0)
    folded = (affinity, panel_unit, kept_rec)
    affinity, all_unit, all_rec = folded
    my_index = lax.axis_index("wide")
    above = my_index * SEG_DEV - 1
    below = my_index * SEG_DEV + SEG_DEV
    above_safe = jnp.clip(above, 0, total_rows - 1)
    below_safe = jnp.clip(below, 0, total_rows - 1)
    edge_unit = jnp.concatenate(
        [
            lax.dynamic_slice_in_dim(all_unit, above_safe, 1, 0),
            lax.dynamic_slice_in_dim(all_unit, below_safe, 1, 0),
        ],
        axis=0,
    )
    edge_rec = jnp.concatenate(
        [
            lax.dynamic_slice_in_dim(all_rec, above_safe, 1, 0),
            lax.dynamic_slice_in_dim(all_rec, below_safe, 1, 0),
        ],
        axis=0,
    )
    edge_rows = score_panel(edge_unit, edge_rec, all_unit, all_rec)
    inside = jnp.stack([above >= 0, below < total_rows])
    edge_rows = jnp.where(inside[:, None], edge_rows, 0.0)
    padded = jnp.concatenate([edge_rows[0:1], affinity, edge_rows[1:2]], axis=0)
    return smooth_rows(padded, smooth_kernel)


def solution(mesh):
    in_specs = (
        P(("parts", "wide"), None),
        P(("parts", "wide")),
        P(("parts", "wide")),
        P(("parts", "wide")),
        P(),
        P(),
        P(),
        P(),
    )
    out_specs = P(("parts", "wide"), None)
    return jax.shard_map(
        per_device, mesh=mesh, in_specs=in_specs, out_specs=out_specs, check_vma=False
    )
```

profile of v0, /device:TPU:0, one launch (start us, length us, event | category | flops | bytes accessed | tf_op | source)
XLA Modules:
  0.0 302.0 jit_solution(8323069585257110534)
XLA Ops:
  3.2 7.4 %all-to-all-start = ((s32[16,1,4]{2,1,0:T(1,128)}), s32[16,1,4]{2,1,0:T(1,128)S(1)}, u32[]{:S(2)}, u32[]{:S(2)}) async-start(s32[16,1,4]{2,1,0:T(1,128)} %bitcast.7), calls=%async_computation | async-start | bytes 16384 | tf_op jit(solution)/shard_map/all_to_all | solution.py:97
  11.3 178.5 %while.12 = (s32[]{:T(128)}, f32[2048,80]{0,1:T(8,128)}, s32[64,2]{0,1:T(2,128)S(1)}, f32[64,66,80]{1,2,0:T(8,128)}, s32[]{:T(128)}) while((s32[]{:T(128)}, f32[2048,80]{0,1:T(8,128)}, s32[64,2]{0,1:T(2,128)S(1)}, f32[64,66,80]{1,2,0:T(8,128)}, s32[]{:T(128)}) %tuple.54), condition=%wide.while_cond, body=%wide.while_body.sunk | while | flops 2 | bytes 82533 | solution.py:90
  25.9 2.2 bitcast_dynamic-update-slice_fusion.2
  39.8 2.2 bitcast_dynamic-update-slice_fusion.2
  79.0 2.2 bitcast_dynamic-update-slice_fusion.2
  104.0 2.2 bitcast_dynamic-update-slice_fusion.2
  112.4 2.2 bitcast_dynamic-update-slice_fusion.2
  145.7 2.2 bitcast_dynamic-update-slice_fusion.2
  148.5 2.2 bitcast_dynamic-update-slice_fusion.2
  151.3 2.2 bitcast_dynamic-update-slice_fusion.2
  156.9 2.2 bitcast_dynamic-update-slice_fusion.2
  176.4 2.2 bitcast_dynamic-update-slice_fusion.2
  179.2 2.2 bitcast_dynamic-update-slice_fusion.2
  189.8 3.3 %copy.18 = f32[4,16,66,80]{3,2,1,0:T(8,128)} copy(f32[4,16,66,80]{2,3,1,0:T(8,128)} %bitcast.62) | data formatting | bytes 2703360 | tf_op jit(solution)/shard_map/while | solution.py:38
  193.1 26.8 %while.11 = (s32[]{:T(128)}, f32[4,16,2048]{2,1,0:T(8,128)S(1)}, f32[4,16,66,80]{3,2,1,0:T(8,128)}, f32[240,1024]{1,0:T(8,128)S(1)}, f32[1024]{0:T(1024)S(1)}, /*index=5*/s32[]{:T(128)}) while((s32[]{:T(128)}, f32[4,16,2048]{2,1,0:T(8,128)S(1)}, f32[4,16,66,80]{3,2,1,0:T(8,128)}, f32[240,1024]{1,0:T(8,128)S(1)}, f32[1024]{0:T(1024)S(1)}, ...), condition=%wide.region_8.9_spmd, body=%wide.region_5.8_spmd.sunk | while | flops 3028828160 | bytes 15691861 | solution.py:38
  194.9 4.0 %bitcast_reduce_fusion.2 = (f32[16,1024]{1,0:T(8,128)S(1)}, f32[1024,1024]{1,0:T(8,128)S(1)}) fusion(f32[1024]{0:T(1024)S(1)} %get-tuple-element.202, f32[1024,240]{1,0:T(8,128)S(1)} %bitcast.61, f32[240,1024]{1,0:T(8,128)S(1)} %get-tuple-element.201), kind=kOutput, calls=%fused_computation.1.clone.1 | convolution fusion | flops 3023028224 | bytes 6230016 | tf_op jit(solution)/shard_map/while/body/eval_jaxpr/dot_general | solution.py:26
  201.6 4.0 %bitcast_reduce_fusion.2 = (f32[16,1024]{1,0:T(8,128)S(1)}, f32[1024,1024]{1,0:T(8,128)S(1)}) fusion(f32[1024]{0:T(1024)S(1)} %get-tuple-element.202, f32[1024,240]{1,0:T(8,128)S(1)} %bitcast.61, f32[240,1024]{1,0:T(8,128)S(1)} %get-tuple-element.201), kind=kOutput, calls=%fused_computation.1.clone.1 | convolution fusion | flops 3023028224 | bytes 6230016 | tf_op jit(solution)/shard_map/while/body/eval_jaxpr/dot_general | solution.py:26
  208.3 4.0 %bitcast_reduce_fusion.2 = (f32[16,1024]{1,0:T(8,128)S(1)}, f32[1024,1024]{1,0:T(8,128)S(1)}) fusion(f32[1024]{0:T(1024)S(1)} %get-tuple-element.202, f32[1024,240]{1,0:T(8,128)S(1)} %bitcast.61, f32[240,1024]{1,0:T(8,128)S(1)} %get-tuple-element.201), kind=kOutput, calls=%fused_computation.1.clone.1 | convolution fusion | flops 3023028224 | bytes 6230016 | tf_op jit(solution)/shard_map/while/body/eval_jaxpr/dot_general | solution.py:26
  215.0 4.0 %bitcast_reduce_fusion.2 = (f32[16,1024]{1,0:T(8,128)S(1)}, f32[1024,1024]{1,0:T(8,128)S(1)}) fusion(f32[1024]{0:T(1024)S(1)} %get-tuple-element.202, f32[1024,240]{1,0:T(8,128)S(1)} %bitcast.61, f32[240,1024]{1,0:T(8,128)S(1)} %get-tuple-element.201), kind=kOutput, calls=%fused_computation.1.clone.1 | convolution fusion | flops 3023028224 | bytes 6230016 | tf_op jit(solution)/shard_map/while/body/eval_jaxpr/dot_general | solution.py:26
  224.5 6.3 %all-to-all-start.1 = ((f32[16,4,192]{2,1,0:T(4,128)}), f32[16,4,192]{2,1,0:T(4,128)S(1)}, u32[]{:S(2)}, u32[]{:S(2)}) async-start(f32[16,4,192]{2,1,0:T(4,128)} %reshape.108), calls=%async_computation.1 | async-start | bytes 131072 | tf_op jit(solution)/shard_map/all_to_all | solution.py:96
  232.9 12.4 %all-reduce.2 = s32[512]{0:T(512)S(1)} all-reduce(s32[512]{0:T(512)S(1)} %dynamic-update-slice.2), channel_id=1, replica_groups=mesh['parts'=2,'wide'=16] {'wide'}, use_global_device_ids=true, to_apply=%add.2 | all-reduce | flops 512 | bytes 4096
  247.5 29.5 %psum.7 = f32[192]{0:T(256)S(1)} all-reduce(f32[192]{0:T(256)S(1)} %get-tuple-element.101), channel_id=1, replica_groups=mesh['parts'=2,'wide'=16] {'wide'}, use_global_device_ids=true, to_apply=%region_10.11 | all-reduce | flops 192 | bytes 1536 | tf_op jit(solution)/shard_map/psum | solution.py:101
  277.2 17.9 %all_gather.7 = bf16[512,192]{1,0:T(8,128)(2,1)S(1)} all-gather(bf16[32,192]{1,0:T(8,128)(2,1)S(1)} %divide_convert_fusion), channel_id=1, replica_groups=mesh['parts'=2,'wide'=16] {'wide'}, dimensions={0}, use_global_device_ids=true | all-gather | bytes 208896 | tf_op jit(solution)/shard_map/all_gather | solution.py:109
  295.7 6.3 %fusion.7 = f32[32,512]{1,0:T(8,128)} fusion(f32[34,514]{1,0:T(8,128)S(1)} %select_maximum_fusion, f32[1,512]{1,0:T(1,128)S(1)} %get-tuple-element.89, f32[32,512]{1,0:T(8,128)S(1)} %fusion.3, f32[1,512]{1,0:T(1,128)S(1)} %get-tuple-element.88, f32[]{:T(128)} %bitcast.19, f32[]{:T(128)} %bitcast.18, f32[]{:T(128)} %bitcast.17, f32[]{:T(128)} %bitcast.16, ...), kind=kLoop, calls=%fused_computation.24 | loop fusion | flops 311296 | bytes 528420 | tf_op jit(solution)/shard_map/add | solution.py:50
  (261 shorter events, 177.2 us)
Async XLA Ops:
  0.0 220.0 %copy-start = (f32[2048,192]{0,1:T(8,128)S(1)}, f32[2048,192]{0,1:T(8,128)}, u32[]{:S(2)}) copy-start(f32[2048,192]{0,1:T(8,128)} %param.16) | copy-start | bytes 4718596
  0.0 193.1 %copy-start.1 = (f32[240,1024]{1,0:T(8,128)S(1)}, f32[240,1024]{1,0:T(8,128)}, u32[]{:S(2)}) copy-start(f32[240,1024]{1,0:T(8,128)} %param.14) | copy-start | bytes 2949124
  0.0 193.1 %copy-start.2 = (f32[1024]{0:T(1024)S(1)}, f32[1024]{0:T(1024)}, u32[]{:S(2)}) copy-start(f32[1024]{0:T(1024)} %param.15) | copy-start | bytes 12292
  3.2 221.3 %all-to-all-start = ((s32[16,1,4]{2,1,0:T(1,128)}), s32[16,1,4]{2,1,0:T(1,128)S(1)}, u32[]{:S(2)}, u32[]{:S(2)}) async-start(s32[16,1,4]{2,1,0:T(1,128)} %bitcast.7), calls=%async_computation | async-start | bytes 16384 | tf_op jit(solution)/shard_map/all_to_all | solution.py:97
  193.1 29.3 %copy-start.3 = (f32[3,3]{1,0:T(4,128)S(1)}, f32[3,3]{1,0:T(4,128)}, u32[]{:S(2)}) copy-start(f32[3,3]{1,0:T(4,128)} %param.17) | copy-start | bytes 112
  193.1 30.1 %copy-start.4 = (u32[32]{0:T(128)S(1)}, u32[32]{0:T(128)}, u32[]{:S(2)}) copy-start(u32[32]{0:T(128)} %constant.91) | copy-start | bytes 388
  224.5 22.9 %all-to-all-start.1 = ((f32[16,4,192]{2,1,0:T(4,128)}), f32[16,4,192]{2,1,0:T(4,128)S(1)}, u32[]{:S(2)}, u32[]{:S(2)}) async-start(f32[16,4,192]{2,1,0:T(4,128)} %reshape.108), calls=%async_computation.1 | async-start | bytes 131072 | tf_op jit(solution)/shard_map/all_to_all | solution.py:96
where the time goes:
time: 306 us; the launch traced here: 302 us
  local copies, waits for them, and re-layouts  191 us (62%)
  blocking collectives  59.8 us (20%)
  matrix products  18.5 us (6%)
  other arithmetic  17.7 us (6%)
  starting transfers between devices  13.7 us (4%)
    gather x192, local copies, waits for them, and re-layouts  178 us
    psum x1, blocking collectives, per_device(): mean_sum = lax.psum(jnp.sum(seg_rows, axis=0), 'wide')  29.5 us
    all_gather x1, blocking collectives, per_device(): panel_unit = lax.all_gather(unit, 'wide', axis=0, tiled=True)  17.9 us
    dot_general x4, matrix products, one_block(): jnp.dot(stacked.reshape(block_size * SEGLEN, 3 * FEAT), conv_weight, prec...  16.2 us
    unnamed x1, blocking collectives  12.4 us
    all_to_all x1, starting transfers between devices, per_device(): lax.all_to_all(send_rec, 'wide', split_axis=0, concat_axis=0, tiled=True)  7.39 us
    all_to_all x1, starting transfers between devices, per_device(): lax.all_to_all(outgoing, 'wide', split_axis=0, concat_axis=0, tiled=True)  6.35 us
    add x1, other arithmetic, smooth_rows(): result + smooth_kernel[row_off, col_off] * padded[row_off:row_off + heigh...  6.29 us
  transfers between devices with their start and end apart: 2, of which 0 were waited for; matrix products, arithmetic and copies ran while one was open for 72% of the time, Pallas kernels for 0%

commit v1 on v0

--- a/solution.py
+++ b/solution.py
@@ -106,7 +106,21 @@
     total_rows = SEG_DEV * group_size
     all_rec = jnp.zeros((total_rows,), jnp.int32)
     kept_rec = all_rec
-    panel_unit = lax.all_gather(unit, "wide", axis=0, tiled=True)
+    ways, here, step = (lax.axis_size("wide"), lax.axis_index("wide"), unit.shape[0])
+    shape = [n * ways if d == 0 else n for d, n in enumerate(unit.shape)]
+    full = lax.dynamic_update_slice_in_dim(jnp.zeros(shape, unit.dtype), unit, here * step, axis=0)
+    going_up = going_down = unit
+    for far in range(1, ways // 2 + 1):
+        going_up = lax.ppermute(going_up, "wide", [(d, (d + 1) % ways) for d in range(ways)])
+        full = lax.dynamic_update_slice_in_dim(full, going_up, (here - far) % ways * step, axis=0)
+        if 2 * far < ways:
+            going_down = lax.ppermute(
+                going_down, "wide", [(d, (d - 1) % ways) for d in range(ways)]
+            )
+            full = lax.dynamic_update_slice_in_dim(
+                full, going_down, (here + far) % ways * step, axis=0
+            )
+    panel_unit = full
     panel_rec = lax.all_gather(seg_rec, "wide", axis=0, tiled=True)
     scores = score_panel(unit, seg_rec, panel_unit, panel_rec)
     affinity = scores

time: 306 us -> 338 us (1.10)
  starting transfers between devices: 13.7 us -> 44.7 us
  blocking collectives: 59.8 us -> 41.9 us
  waiting for transfers between devices: 0.01 us -> 14.5 us
  local copies, waits for them, and re-layouts: 191 us -> 196 us
    ppermute x0 -> x15, starting transfers between devices: none -> 31 us  [the longest x7 30.9 us: per_device(): lax.ppermute(going_down, 'wide', [(d, (d - 1) % ways) for d in range(ways)])]
    all_gather x1 -> x0, blocking collectives: 17.9 us -> none  [per_device(): panel_unit = lax.all_gather(unit, 'wide', axis=0, tiled=True)]
    ppermute x0 -> x15, waiting for transfers between devices: none -> 14.5 us  [the longest x8 14.3 us: per_device(): lax.ppermute(going_up, 'wide', [(d, (d + 1) % ways) for d in range(ways)])]
    gather x192, local copies, waits for them, and re-layouts: 178 us -> 183 us
  transfers between devices with their start and end apart: 2 -> 17, of which waited for: 0 -> 7; matrix products, arithmetic and copies ran while one was open for 72% -> 66% of each run, Pallas kernels for 0% -> 0%
where the time goes in v1:
time: 338 us; the launch traced here: 335 us
  local copies, waits for them, and re-layouts  196 us (58%)
  starting transfers between devices  44.7 us (13%)
  blocking collectives  41.9 us (12%)
  matrix products  18.3 us (5%)
  other arithmetic  17.7 us (5%)
  waiting for transfers between devices  14.5 us (4%)
    gather x192, local copies, waits for them, and re-layouts  183 us
    ppermute x7, starting transfers between devices, per_device(): lax.ppermute(going_down, 'wide', [(d, (d - 1) % ways) for d in range(ways)])  30.9 us
    psum x1, blocking collectives, per_device(): mean_sum = lax.psum(jnp.sum(seg_rows, axis=0), 'wide')  29.5 us
    dot_general x4, matrix products, one_block(): jnp.dot(stacked.reshape(block_size * SEGLEN, 3 * FEAT), conv_weight, prec...  16 us
    ppermute x8, waiting for transfers between devices, per_device(): lax.ppermute(going_up, 'wide', [(d, (d + 1) % ways) for d in range(ways)])  14.3 us
    unnamed x1, blocking collectives  12.4 us
    all_to_all x1, starting transfers between devices, per_device(): lax.all_to_all(send_rec, 'wide', split_axis=0, concat_axis=0, tiled=True)  7.39 us
  transfers between devices with their start and end apart: 17, of which 7 were waited for; matrix products, arithmetic and copies ran while one was open for 66% of the time, Pallas kernels for 0%

profile of v1, /device:TPU:0, one launch (start us, length us, event | category | flops | bytes accessed | tf_op | source)
XLA Modules:
  0.0 334.6 jit_solution(13710289483722801164)
XLA Ops:
  3.2 7.4 %all-to-all-start = ((s32[16,1,4]{2,1,0:T(1,128)}), s32[16,1,4]{2,1,0:T(1,128)S(1)}, u32[]{:S(2)}, u32[]{:S(2)}) async-start(s32[16,1,4]{2,1,0:T(1,128)} %bitcast.7), calls=%async_computation | async-start | bytes 16384 | tf_op jit(solution)/shard_map/all_to_all | solution.py:97
  11.6 183.4 %while.12 = (s32[]{:T(128)}, f32[2048,80]{0,1:T(8,128)}, s32[64,2]{0,1:T(2,128)S(1)}, f32[64,66,80]{1,2,0:T(8,128)}, s32[]{:T(128)}) while((s32[]{:T(128)}, f32[2048,80]{0,1:T(8,128)}, s32[64,2]{0,1:T(2,128)S(1)}, f32[64,66,80]{1,2,0:T(8,128)}, s32[]{:T(128)}) %tuple.55), condition=%wide.while_cond, body=%wide.while_body.sunk | while | flops 2 | bytes 83033 | solution.py:90
  40.9 2.2 bitcast_dynamic-update-slice_fusion.2
  152.5 2.2 bitcast_dynamic-update-slice_fusion.2
  161.1 2.2 bitcast_dynamic-update-slice_fusion.2
  181.2 2.2 bitcast_dynamic-update-slice_fusion.2
  195.0 3.3 copy.18
  198.3 26.7 %while.11 = (s32[]{:T(128)}, f32[4,16,2048]{2,1,0:T(8,128)S(1)}, f32[4,16,66,80]{3,2,1,0:T(8,128)}, f32[240,1024]{1,0:T(8,128)S(1)}, f32[1024]{0:T(1024)S(1)}, /*index=5*/s32[]{:T(128)}) while((s32[]{:T(128)}, f32[4,16,2048]{2,1,0:T(8,128)S(1)}, f32[4,16,66,80]{3,2,1,0:T(8,128)}, f32[240,1024]{1,0:T(8,128)S(1)}, f32[1024]{0:T(1024)S(1)}, ...), condition=%wide.region_8.9_spmd, body=%wide.region_5.8_spmd.sunk | while | flops 3028828160 | bytes 15691853 | solution.py:38
  200.0 4.0 %bitcast_reduce_fusion.2 = (f32[16,1024]{1,0:T(8,128)S(1)}, f32[1024,1024]{1,0:T(8,128)S(1)}) fusion(f32[1024]{0:T(1024)S(1)} %get-tuple-element.204, f32[1024,240]{1,0:T(8,128)S(1)} %bitcast.61, f32[240,1024]{1,0:T(8,128)S(1)} %get-tuple-element.203), kind=kOutput, calls=%fused_computation.1.clone.1 | convolution fusion | flops 3023028224 | bytes 6230016 | tf_op jit(solution)/shard_map/while/body/eval_jaxpr/dot_general | solution.py:26
  206.7 4.0 %bitcast_reduce_fusion.2 = (f32[16,1024]{1,0:T(8,128)S(1)}, f32[1024,1024]{1,0:T(8,128)S(1)}) fusion(f32[1024]{0:T(1024)S(1)} %get-tuple-element.204, f32[1024,240]{1,0:T(8,128)S(1)} %bitcast.61, f32[240,1024]{1,0:T(8,128)S(1)} %get-tuple-element.203), kind=kOutput, calls=%fused_computation.1.clone.1 | convolution fusion | flops 3023028224 | bytes 6230016 | tf_op jit(solution)/shard_map/while/body/eval_jaxpr/dot_general | solution.py:26
  213.4 4.0 %bitcast_reduce_fusion.2 = (f32[16,1024]{1,0:T(8,128)S(1)}, f32[1024,1024]{1,0:T(8,128)S(1)}) fusion(f32[1024]{0:T(1024)S(1)} %get-tuple-element.204, f32[1024,240]{1,0:T(8,128)S(1)} %bitcast.61, f32[240,1024]{1,0:T(8,128)S(1)} %get-tuple-element.203), kind=kOutput, calls=%fused_computation.1.clone.1 | convolution fusion | flops 3023028224 | bytes 6230016 | tf_op jit(solution)/shard_map/while/body/eval_jaxpr/dot_general | solution.py:26
  220.1 4.0 %bitcast_reduce_fusion.2 = (f32[16,1024]{1,0:T(8,128)S(1)}, f32[1024,1024]{1,0:T(8,128)S(1)}) fusion(f32[1024]{0:T(1024)S(1)} %get-tuple-element.204, f32[1024,240]{1,0:T(8,128)S(1)} %bitcast.61, f32[240,1024]{1,0:T(8,128)S(1)} %get-tuple-element.203), kind=kOutput, calls=%fused_computation.1.clone.1 | convolution fusion | flops 3023028224 | bytes 6230016 | tf_op jit(solution)/shard_map/while/body/eval_jaxpr/dot_general | solution.py:26
  229.5 6.3 %all-to-all-start.1 = ((f32[16,4,192]{2,1,0:T(4,128)}), f32[16,4,192]{2,1,0:T(4,128)S(1)}, u32[]{:S(2)}, u32[]{:S(2)}) async-start(f32[16,4,192]{2,1,0:T(4,128)} %reshape.108), calls=%async_computation.1 | async-start | bytes 131072 | tf_op jit(solution)/shard_map/all_to_all | solution.py:96
  237.9 12.4 %all-reduce.2 = s32[512]{0:T(512)S(1)} all-reduce(s32[512]{0:T(512)S(1)} %dynamic-update-slice.2), channel_id=1, replica_groups=mesh['parts'=2,'wide'=16] {'wide'}, use_global_device_ids=true, to_apply=%add.2 | all-reduce | flops 512 | bytes 4096
  251.2 29.5 %psum.7 = f32[192]{0:T(256)S(1)} all-reduce(f32[192]{0:T(256)S(1)} %get-tuple-element.103), channel_id=1, replica_groups=mesh['parts'=2,'wide'=16] {'wide'}, use_global_device_ids=true, to_apply=%region_10.11 | all-reduce | flops 192 | bytes 1536 | tf_op jit(solution)/shard_map/psum | solution.py:101
  280.9 4.4 %collective-permute-start.1 = (bf16[32,192]{1,0:T(8,128)(2,1)S(1)}, bf16[32,192]{1,0:T(8,128)(2,1)S(1)}, u32[]{:S(2)}, u32[]{:S(2)}) collective-permute-start(bf16[32,192]{1,0:T(8,128)(2,1)S(1)} %get-tuple-element.82), channel_id=1, source_target_pairs={{0,15},{1,0},{2,1},{3,2},{4,3},{5,4},{6,5},{7,6},{8,7},{9,8},{10,9... | collective-permute-start | bytes 36872 | tf_op jit(solution)/shard_map/ppermute | solution.py:117
  286.8 4.4 %collective-permute-start.3 = (bf16[32,192]{1,0:T(8,128)(2,1)S(1)}, bf16[32,192]{1,0:T(8,128)(2,1)S(1)}, u32[]{:S(2)}, u32[]{:S(2)}) collective-permute-start(bf16[32,192]{1,0:T(8,128)(2,1)S(1)} %collective-permute-done.1), channel_id=1, source_target_pairs={{0,15},{1,0},{2,1},{3,2},{4,3},{5,4},{6,5},{7,6},{8,7},{9,8},{10,9... | collective-permute-start | bytes 36872 | tf_op jit(solution)/shard_map/ppermute | solution.py:117
  292.7 4.4 %collective-permute-start.5 = (bf16[32,192]{1,0:T(8,128)(2,1)S(1)}, bf16[32,192]{1,0:T(8,128)(2,1)S(1)}, u32[]{:S(2)}, u32[]{:S(2)}) collective-permute-start(bf16[32,192]{1,0:T(8,128)(2,1)S(1)} %collective-permute-done.3), channel_id=1, source_target_pairs={{0,15},{1,0},{2,1},{3,2},{4,3},{5,4},{6,5},{7,6},{8,7},{9,8},{10,9... | collective-permute-start | bytes 36872 | tf_op jit(solution)/shard_map/ppermute | solution.py:117
  298.5 4.4 %collective-permute-start.7 = (bf16[32,192]{1,0:T(8,128)(2,1)S(1)}, bf16[32,192]{1,0:T(8,128)(2,1)S(1)}, u32[]{:S(2)}, u32[]{:S(2)}) collective-permute-start(bf16[32,192]{1,0:T(8,128)(2,1)S(1)} %collective-permute-done.5), channel_id=1, source_target_pairs={{0,15},{1,0},{2,1},{3,2},{4,3},{5,4},{6,5},{7,6},{8,7},{9,8},{10,9... | collective-permute-start | bytes 36872 | tf_op jit(solution)/shard_map/ppermute | solution.py:117
  304.4 4.4 %collective-permute-start.9 = (bf16[32,192]{1,0:T(8,128)(2,1)S(1)}, bf16[32,192]{1,0:T(8,128)(2,1)S(1)}, u32[]{:S(2)}, u32[]{:S(2)}) collective-permute-start(bf16[32,192]{1,0:T(8,128)(2,1)S(1)} %collective-permute-done.7), channel_id=1, source_target_pairs={{0,15},{1,0},{2,1},{3,2},{4,3},{5,4},{6,5},{7,6},{8,7},{9,8},{10,9... | collective-permute-start | bytes 36872 | tf_op jit(solution)/shard_map/ppermute | solution.py:117
  310.3 4.4 %collective-permute-start.11 = (bf16[32,192]{1,0:T(8,128)(2,1)S(1)}, bf16[32,192]{1,0:T(8,128)(2,1)S(1)}, u32[]{:S(2)}, u32[]{:S(2)}) collective-permute-start(bf16[32,192]{1,0:T(8,128)(2,1)S(1)} %collective-permute-done.9), channel_id=1, source_target_pairs={{0,15},{1,0},{2,1},{3,2},{4,3},{5,4},{6,5},{7,6},{8,7},{9,8},{10,9... | collective-permute-start | bytes 36872 | tf_op jit(solution)/shard_map/ppermute | solution.py:117
  316.1 4.4 %collective-permute-start.13 = (bf16[32,192]{1,0:T(8,128)(2,1)S(1)}, bf16[32,192]{1,0:T(8,128)(2,1)S(1)}, u32[]{:S(2)}, u32[]{:S(2)}) collective-permute-start(bf16[32,192]{1,0:T(8,128)(2,1)S(1)} %collective-permute-done.11), channel_id=1, source_target_pairs={{0,15},{1,0},{2,1},{3,2},{4,3},{5,4},{6,5},{7,6},{8,7},{9,8},{10,9... | collective-permute-start | bytes 36872 | tf_op jit(solution)/shard_map/ppermute | solution.py:117
  322.0 5.8 %collective-permute-done.14 = bf16[32,192]{1,0:T(8,128)(2,1)S(1)} collective-permute-done((bf16[32,192]{1,0:T(8,128)(2,1)S(1)}, bf16[32,192]{1,0:T(8,128)(2,1)S(1)}, u32[]{:S(2)}, u32[]{:S(2)}) %collective-permute-start.14) | collective-permute-done | bytes 12320 | tf_op jit(solution)/shard_map/ppermute | solution.py:114
  328.3 6.3 %fusion.7 = f32[32,512]{1,0:T(8,128)} fusion(f32[34,514]{1,0:T(8,128)S(1)} %select_maximum_fusion, f32[1,512]{1,0:T(1,128)S(1)} %get-tuple-element.91, f32[32,512]{1,0:T(8,128)S(1)} %fusion.3, f32[1,512]{1,0:T(1,128)S(1)} %get-tuple-element.90, f32[]{:T(128)} %bitcast.19, f32[]{:T(128)} %bitcast.18, f32[]{:T(128)} %bitcast.17, f32[]{:T(128)} %bitcast.16, ...), kind=kLoop, calls=%fused_computation.24 | loop fusion | flops 311296 | bytes 528420 | tf_op jit(solution)/shard_map/add | solution.py:50
  (306 shorter events, 206.3 us)
Async XLA Ops:
  0.0 225.0 %copy-start = (f32[2048,192]{0,1:T(8,128)S(1)}, f32[2048,192]{0,1:T(8,128)}, u32[]{:S(2)}) copy-start(f32[2048,192]{0,1:T(8,128)} %param.16) | copy-start | bytes 4718596
  0.0 198.2 %copy-start.1 = (f32[240,1024]{1,0:T(8,128)S(1)}, f32[240,1024]{1,0:T(8,128)}, u32[]{:S(2)}) copy-start(f32[240,1024]{1,0:T(8,128)} %param.14) | copy-start | bytes 2949124
  0.0 198.2 %copy-start.2 = (f32[1024]{0:T(1024)S(1)}, f32[1024]{0:T(1024)}, u32[]{:S(2)}) copy-start(f32[1024]{0:T(1024)} %param.15) | copy-start | bytes 12292
  3.2 226.3 %all-to-all-start = ((s32[16,1,4]{2,1,0:T(1,128)}), s32[16,1,4]{2,1,0:T(1,128)S(1)}, u32[]{:S(2)}, u32[]{:S(2)}) async-start(s32[16,1,4]{2,1,0:T(1,128)} %bitcast.7), calls=%async_computation | async-start | bytes 16384 | tf_op jit(solution)/shard_map/all_to_all | solution.py:97
  198.2 29.3 %copy-start.3 = (f32[3,3]{1,0:T(4,128)S(1)}, f32[3,3]{1,0:T(4,128)}, u32[]{:S(2)}) copy-start(f32[3,3]{1,0:T(4,128)} %param.17) | copy-start | bytes 112
  198.2 30.0 %copy-start.4 = (u32[32]{0:T(128)S(1)}, u32[32]{0:T(128)}, u32[]{:S(2)}) copy-start(u32[32]{0:T(128)} %constant.188) | copy-start | bytes 388
  229.5 21.5 %all-to-all-start.1 = ((f32[16,4,192]{2,1,0:T(4,128)}), f32[16,4,192]{2,1,0:T(4,128)S(1)}, u32[]{:S(2)}, u32[]{:S(2)}) async-start(f32[16,4,192]{2,1,0:T(4,128)} %reshape.108), calls=%async_computation.1 | async-start | bytes 131072 | tf_op jit(solution)/shard_map/all_to_all | solution.py:96
  280.9 5.9 %collective-permute-start = (bf16[32,192]{1,0:T(8,128)(2,1)S(1)}, bf16[32,192]{1,0:T(8,128)(2,1)S(1)}, u32[]{:S(2)}, u32[]{:S(2)}) collective-permute-start(bf16[32,192]{1,0:T(8,128)(2,1)S(1)} %get-tuple-element.82), channel_id=1, source_target_pairs={{0,1},{1,2},{2,3},{3,4},{4,5},{5,6},{6,7},{7,8},{8,9},{9,10},{10,1... | collective-permute-start | bytes 36872 | tf_op jit(solution)/shard_map/ppermute | solution.py:114
  280.9 5.9 %collective-permute-start.1 = (bf16[32,192]{1,0:T(8,128)(2,1)S(1)}, bf16[32,192]{1,0:T(8,128)(2,1)S(1)}, u32[]{:S(2)}, u32[]{:S(2)}) collective-permute-start(bf16[32,192]{1,0:T(8,128)(2,1)S(1)} %get-tuple-element.82), channel_id=1, source_target_pairs={{0,15},{1,0},{2,1},{3,2},{4,3},{5,4},{6,5},{7,6},{8,7},{9,8},{10,9... | collective-permute-start | bytes 36872 | tf_op jit(solution)/shard_map/ppermute | solution.py:117
  286.8 5.9 %collective-permute-start.2 = (bf16[32,192]{1,0:T(8,128)(2,1)S(1)}, bf16[32,192]{1,0:T(8,128)(2,1)S(1)}, u32[]{:S(2)}, u32[]{:S(2)}) collective-permute-start(bf16[32,192]{1,0:T(8,128)(2,1)S(1)} %collective-permute-done), channel_id=1, source_target_pairs={{0,1},{1,2},{2,3},{3,4},{4,5},{5,6},{6,7},{7,8},{8,9},{9,10},{10,1... | collective-permute-start | bytes 36872 | tf_op jit(solution)/shard_map/ppermute | solution.py:114
  286.8 5.9 %collective-permute-start.3 = (bf16[32,192]{1,0:T(8,128)(2,1)S(1)}, bf16[32,192]{1,0:T(8,128)(2,1)S(1)}, u32[]{:S(2)}, u32[]{:S(2)}) collective-permute-start(bf16[32,192]{1,0:T(8,128)(2,1)S(1)} %collective-permute-done.1), channel_id=1, source_target_pairs={{0,15},{1,0},{2,1},{3,2},{4,3},{5,4},{6,5},{7,6},{8,7},{9,8},{10,9... | collective-permute-start | bytes 36872 | tf_op jit(solution)/shard_map/ppermute | solution.py:117
  292.7 5.9 %collective-permute-start.4 = (bf16[32,192]{1,0:T(8,128)(2,1)S(1)}, bf16[32,192]{1,0:T(8,128)(2,1)S(1)}, u32[]{:S(2)}, u32[]{:S(2)}) collective-permute-start(bf16[32,192]{1,0:T(8,128)(2,1)S(1)} %collective-permute-done.2), channel_id=1, source_target_pairs={{0,1},{1,2},{2,3},{3,4},{4,5},{5,6},{6,7},{7,8},{8,9},{9,10},{10,1... | collective-permute-start | bytes 36872 | tf_op jit(solution)/shard_map/ppermute | solution.py:114
  292.7 5.9 %collective-permute-start.5 = (bf16[32,192]{1,0:T(8,128)(2,1)S(1)}, bf16[32,192]{1,0:T(8,128)(2,1)S(1)}, u32[]{:S(2)}, u32[]{:S(2)}) collective-permute-start(bf16[32,192]{1,0:T(8,128)(2,1)S(1)} %collective-permute-done.3), channel_id=1, source_target_pairs={{0,15},{1,0},{2,1},{3,2},{4,3},{5,4},{6,5},{7,6},{8,7},{9,8},{10,9... | collective-permute-start | bytes 36872 | tf_op jit(solution)/shard_map/ppermute | solution.py:117
  298.5 5.9 %collective-permute-start.6 = (bf16[32,192]{1,0:T(8,128)(2,1)S(1)}, bf16[32,192]{1,0:T(8,128)(2,1)S(1)}, u32[]{:S(2)}, u32[]{:S(2)}) collective-permute-start(bf16[32,192]{1,0:T(8,128)(2,1)S(1)} %collective-permute-done.4), channel_id=1, source_target_pairs={{0,1},{1,2},{2,3},{3,4},{4,5},{5,6},{6,7},{7,8},{8,9},{9,10},{10,1... | collective-permute-start | bytes 36872 | tf_op jit(solution)/shard_map/ppermute | solution.py:114
  298.5 5.9 %collective-permute-start.7 = (bf16[32,192]{1,0:T(8,128)(2,1)S(1)}, bf16[32,192]{1,0:T(8,128)(2,1)S(1)}, u32[]{:S(2)}, u32[]{:S(2)}) collective-permute-start(bf16[32,192]{1,0:T(8,128)(2,1)S(1)} %collective-permute-done.5), channel_id=1, source_target_pairs={{0,15},{1,0},{2,1},{3,2},{4,3},{5,4},{6,5},{7,6},{8,7},{9,8},{10,9... | collective-permute-start | bytes 36872 | tf_op jit(solution)/shard_map/ppermute | solution.py:117
  304.4 5.9 %collective-permute-start.8 = (bf16[32,192]{1,0:T(8,128)(2,1)S(1)}, bf16[32,192]{1,0:T(8,128)(2,1)S(1)}, u32[]{:S(2)}, u32[]{:S(2)}) collective-permute-start(bf16[32,192]{1,0:T(8,128)(2,1)S(1)} %collective-permute-done.6), channel_id=1, source_target_pairs={{0,1},{1,2},{2,3},{3,4},{4,5},{5,6},{6,7},{7,8},{8,9},{9,10},{10,1... | collective-permute-start | bytes 36872 | tf_op jit(solution)/shard_map/ppermute | solution.py:114
  304.4 5.9 %collective-permute-start.9 = (bf16[32,192]{1,0:T(8,128)(2,1)S(1)}, bf16[32,192]{1,0:T(8,128)(2,1)S(1)}, u32[]{:S(2)}, u32[]{:S(2)}) collective-permute-start(bf16[32,192]{1,0:T(8,128)(2,1)S(1)} %collective-permute-done.7), channel_id=1, source_target_pairs={{0,15},{1,0},{2,1},{3,2},{4,3},{5,4},{6,5},{7,6},{8,7},{9,8},{10,9... | collective-permute-start | bytes 36872 | tf_op jit(solution)/shard_map/ppermute | solution.py:117
  310.2 5.9 %collective-permute-start.10 = (bf16[32,192]{1,0:T(8,128)(2,1)S(1)}, bf16[32,192]{1,0:T(8,128)(2,1)S(1)}, u32[]{:S(2)}, u32[]{:S(2)}) collective-permute-start(bf16[32,192]{1,0:T(8,128)(2,1)S(1)} %collective-permute-done.8), channel_id=1, source_target_pairs={{0,1},{1,2},{2,3},{3,4},{4,5},{5,6},{6,7},{7,8},{8,9},{9,10},{10,1... | collective-permute-start | bytes 36872 | tf_op jit(solution)/shard_map/ppermute | solution.py:114
  310.3 5.9 %collective-permute-start.11 = (bf16[32,192]{1,0:T(8,128)(2,1)S(1)}, bf16[32,192]{1,0:T(8,128)(2,1)S(1)}, u32[]{:S(2)}, u32[]{:S(2)}) collective-permute-start(bf16[32,192]{1,0:T(8,128)(2,1)S(1)} %collective-permute-done.9), channel_id=1, source_target_pairs={{0,15},{1,0},{2,1},{3,2},{4,3},{5,4},{6,5},{7,6},{8,7},{9,8},{10,9... | collective-permute-start | bytes 36872 | tf_op jit(solution)/shard_map/ppermute | solution.py:117
  316.1 5.9 %collective-permute-start.12 = (bf16[32,192]{1,0:T(8,128)(2,1)S(1)}, bf16[32,192]{1,0:T(8,128)(2,1)S(1)}, u32[]{:S(2)}, u32[]{:S(2)}) collective-permute-start(bf16[32,192]{1,0:T(8,128)(2,1)S(1)} %collective-permute-done.10), channel_id=1, source_target_pairs={{0,1},{1,2},{2,3},{3,4},{4,5},{5,6},{6,7},{7,8},{8,9},{9,10},{10,1... | collective-permute-start | bytes 36872 | tf_op jit(solution)/shard_map/ppermute | solution.py:114
  316.1 5.9 %collective-permute-start.13 = (bf16[32,192]{1,0:T(8,128)(2,1)S(1)}, bf16[32,192]{1,0:T(8,128)(2,1)S(1)}, u32[]{:S(2)}, u32[]{:S(2)}) collective-permute-start(bf16[32,192]{1,0:T(8,128)(2,1)S(1)} %collective-permute-done.11), channel_id=1, source_target_pairs={{0,15},{1,0},{2,1},{3,2},{4,3},{5,4},{6,5},{7,6},{8,7},{9,8},{10,9... | collective-permute-start | bytes 36872 | tf_op jit(solution)/shard_map/ppermute | solution.py:117
  322.0 5.9 %collective-permute-start.14 = (bf16[32,192]{1,0:T(8,128)(2,1)S(1)}, bf16[32,192]{1,0:T(8,128)(2,1)S(1)}, u32[]{:S(2)}, u32[]{:S(2)}) collective-permute-start(bf16[32,192]{1,0:T(8,128)(2,1)S(1)} %collective-permute-done.12), channel_id=1, source_target_pairs={{0,1},{1,2},{2,3},{3,4},{4,5},{5,6},{6,7},{7,8},{8,9},{9,10},{10,1... | collective-permute-start | bytes 36872 | tf_op jit(solution)/shard_map/ppermute | solution.py:114
